TPU v7x, 512 devices: a whole 4x4x16 slice. The times are simulated.
512 devices in a mesh: blk: 128 (over x, z, y_lo), frq: 4 (over y_hi, core).
Axes of the slice: x: 4, y: 4 (y_hi: 2, y_lo: 2; y = y_hi * 2 + y_lo), z: 16, core: 2. Of those that a mesh axis runs over, the one named last changes fastest.
Arguments:
- spectra: bfloat16 [2, 3, 2048, 512], P(None, None, 'blk', 'frq'), may hold values from -6 to 6
- observed: bfloat16 [32768, 3, 3, 1024], P(('blk', 'frq')), may hold values from -6 to 6
- own_station: int32 [128, 128, 2], P('blk'), may hold values from 0 to 15
- partner_station: int32 [128, 128, 2], P('blk'), may hold values from 0 to 15, as said below
- pair_count: int32 [128, 128], P('blk'), may hold values from 1 to 2, as said below
Outputs:
- adjoint: float32 [1024, 3, 2048], P('frq', None, 'blk')
Inputs may be any that keep to these rules, and one draw needn't show every extreme that they name: `partner_station`: within the reading block's own block pair, a slot's two stations differ. `pair_count`: the live slots of a block pair are its first ones; every reading block has a block pair with all 2 slots live.
All inputs are finite; a program needn't handle non-finite values.
Results may differ from a plain program's by a relative error of at most 0.003.
Values may be sent and summed in bfloat16 or wider, within the bound.
No kernel may reach another device: no remote copies, remote signals or barrier semaphores. Data moves between devices by JAX's collectives and lax.ppermute only.
A program may use at most 64 MiB of HBM per device.

v0:
```python
import math
import jax
import jax.numpy as jnp
from jax import lax
from jax.sharding import PartitionSpec as P

NF = 512
NT = 1024


def phase_table(freq_start, freq_count, time_count):
    freq_index = lax.iota(jnp.int32, freq_count) + freq_start
    time_index = lax.iota(jnp.int32, time_count)
    phase_num = (2 * freq_index + 1)[:, None] * time_index[None, :] % (2 * NT)
    return phase_num.astype(jnp.float32) * (math.pi / NT)


def lag_window():
    time_index = lax.iota(jnp.int32, NT)
    lag_size = jnp.minimum(time_index, NT - time_index)
    return ((lag_size >= NT // 32) & (lag_size < NT // 4)).astype(jnp.float32)


def cross_spectra(first_rows, second_rows):
    real_part = (
        first_rows[:, 0, :, None] * second_rows[:, 0, None, :]
        + first_rows[:, 1, :, None] * second_rows[:, 1, None, :]
    )
    imag_part = (
        first_rows[:, 1, :, None] * second_rows[:, 0, None, :]
        - first_rows[:, 0, :, None] * second_rows[:, 1, None, :]
    )
    return jnp.stack([real_part, imag_part], axis=3)


def pair_gradients(adjoint_rows, first_rows, second_rows):
    adj_real = adjoint_rows[:, :, :, 0]
    adj_imag = adjoint_rows[:, :, :, 1]
    own_real = jnp.sum(
        adj_real * second_rows[:, 0, None] - adj_imag * second_rows[:, 1, None], axis=2
    )
    own_imag = jnp.sum(
        adj_real * second_rows[:, 1, None] + adj_imag * second_rows[:, 0, None], axis=2
    )
    far_real = jnp.sum(
        adj_real * first_rows[:, 0, :, None] + adj_imag * first_rows[:, 1, :, None], axis=1
    )
    far_imag = jnp.sum(
        adj_real * first_rows[:, 1, :, None] - adj_imag * first_rows[:, 0, :, None], axis=1
    )
    return (jnp.stack([own_real, own_imag], axis=1), jnp.stack([far_real, far_imag], axis=1))


def local(spectra, observed, own_station, partner_station, pair_count):
    block_total = lax.axis_size("blk")
    band_total = lax.axis_size("frq")
    per_block = spectra.shape[2]
    freq_dev = spectra.shape[3]
    slot_cap = own_station.shape[2]
    slot_total = block_total * slot_cap
    item_count = slot_total // band_total
    band_index = lax.axis_index("frq")
    spec_rows = jnp.transpose(spectra, (2, 0, 1, 3))
    own_ids = own_station[0].reshape(slot_total)
    partner_local = partner_station[0]
    partner_ids = partner_local.reshape(slot_total)
    alive_mask = (
        (lax.iota(jnp.int32, slot_cap)[None, :] < pair_count[0][:, None])
        .reshape(slot_total)
        .astype(jnp.float32)
    )
    own_rows = jnp.take(spec_rows, own_ids, axis=0)
    part_rows = lax.all_gather(spec_rows, "blk", axis=0, tiled=True)
    first_row = jnp.int32(0)
    row_count = part_rows.shape[0]
    block_span = min(block_total, -(-row_count // per_block) + 1)
    first_block = jnp.clip(first_row // per_block, 0, block_total - block_span)
    slot_low = first_block * slot_cap
    slot_span = block_span * slot_cap
    block_of_slot = (slot_low + lax.iota(jnp.int32, slot_span)) // slot_cap
    global_ids = block_of_slot * per_block + partner_ids
    inside = (global_ids >= first_row) & (global_ids < first_row + row_count)
    fetched = jnp.take(part_rows, jnp.clip(global_ids, 0, row_count - 1), axis=0)
    fresh = (
        cross_spectra(own_rows.astype(jnp.float32), fetched.astype(jnp.float32))
        * alive_mask[:, None, None, None, None]
    ).astype(jnp.bfloat16)
    cross_old = jnp.zeros((slot_total, 3, 3, 2, freq_dev), jnp.bfloat16)
    rows_old = jnp.zeros((slot_total, 2, 3, freq_dev), jnp.bfloat16)
    cross_new = jnp.where(inside[:, None, None, None, None], fresh, cross_old)
    rows_new = jnp.where(inside[:, None, None, None], fetched, rows_old)
    phase = phase_table(0, NF, NT)
    basis = jnp.concatenate(
        [
            (jnp.cos(phase) / math.sqrt(NF)).astype(jnp.bfloat16),
            -(jnp.sin(phase) / math.sqrt(NF)).astype(jnp.bfloat16),
        ],
        axis=0,
    )
    window = lag_window()
    alive_band = lax.dynamic_slice_in_dim(alive_mask, band_index * item_count, item_count)
    observed_rows = observed.reshape(item_count * 9, NT).astype(jnp.float32)
    station_iota = lax.iota(jnp.int32, per_block)
    sent = cross_new.reshape(band_total, item_count, 3, 3, 2, freq_dev)
    whole_band = lax.all_to_all(sent, "frq", split_axis=0, concat_axis=5, tiled=True)
    correlation = jnp.dot(
        whole_band.reshape(item_count * 9, 2 * NF), basis, preferred_element_type=jnp.float32
    )
    residual = (
        (correlation - observed_rows) * jnp.repeat(alive_band, 9)[:, None] * window[None, :]
    ).astype(jnp.bfloat16)
    adjoint_rows = (
        lax.dot_general(
            residual, basis, (((1,), (1,)), ((), ())), preferred_element_type=jnp.float32
        )
        .astype(jnp.bfloat16)
        .reshape(1, item_count, 3, 3, 2, NF)
    )
    returned = lax.all_to_all(adjoint_rows, "frq", split_axis=5, concat_axis=0, tiled=True).reshape(
        slot_total, 3, 3, 2, freq_dev
    )
    own_grad, far_grad = pair_gradients(
        returned.astype(jnp.float32), own_rows.astype(jnp.float32), rows_new.astype(jnp.float32)
    )
    own_onehot = (own_ids[None, :] == station_iota[:, None]).astype(jnp.float32)
    grad_local = jnp.dot(
        own_onehot,
        own_grad.reshape(slot_total, 6 * freq_dev),
        precision=lax.Precision.HIGHEST,
        preferred_element_type=jnp.float32,
    )
    far_block = far_grad.reshape(block_total, slot_cap, 2, 3, freq_dev)
    back_grad, back_ids = (
        lax.all_to_all(
            far_block.astype(jnp.bfloat16), "blk", split_axis=0, concat_axis=0, tiled=True
        ).astype(far_block.dtype),
        lax.all_to_all(partner_local, "blk", split_axis=0, concat_axis=0, tiled=True),
    )
    back_onehot = (back_ids.reshape(slot_total)[None, :] == station_iota[:, None]).astype(
        jnp.float32
    )
    station_grad = grad_local + jnp.dot(
        back_onehot,
        back_grad.reshape(slot_total, 6 * freq_dev),
        precision=lax.Precision.HIGHEST,
        preferred_element_type=jnp.float32,
    )
    grad_matrix = jnp.transpose(
        station_grad.reshape(per_block, 2, 3, freq_dev), (1, 3, 2, 0)
    ).reshape(2 * freq_dev, 3 * per_block)
    output_scale = 1.0 / math.sqrt(2.0 * block_total * slot_cap / per_block)
    phase_part = phase_table(
        band_index * freq_dev, freq_dev, NT // band_total * lax.axis_size("frq")
    )
    basis_part = jnp.concatenate(
        [jnp.cos(phase_part) / math.sqrt(NF), -(jnp.sin(phase_part) / math.sqrt(NF))], axis=0
    )
    product = lax.dot_general(
        basis_part,
        grad_matrix,
        (((0,), (0,)), ((), ())),
        precision=lax.Precision.HIGHEST,
        preferred_element_type=jnp.float32,
    )
    return lax.psum_scatter(
        product.reshape(NT // band_total * lax.axis_size("frq"), 3, per_block) * output_scale,
        "frq",
        scatter_dimension=0,
        tiled=True,
    )


def solution(mesh):
    return jax.shard_map(
        local,
        mesh=mesh,
        in_specs=(
            P(None, None, "blk", "frq"),
            P(("blk", "frq"), None, None, None),
            P("blk", None, None),
            P("blk", None, None),
            P("blk", None),
        ),
        out_specs=P("frq", None, "blk"),
        check_vma=False,
    )
```

profile of v0, /device:TPU:1, one launch (start us, length us, event | category | flops | bytes accessed | tf_op | source)
XLA Modules:
  0.0 784.7 jit_solution(10995173478806446138)
XLA Ops:
  6.5 1.4 copy.169
  7.9 1.4 copy.126
  13.3 2.2 gather_fusion
  22.4 2.3 copy.142
  24.7 2.6 reshape.280
  27.4 493.7 %all-gather.2.cloned.1.call-done = bf16[2048,2,3,128]{3,1,2,0:T(2,128)(2,1)} async-done(((bf16[16,2,3,128]{3,1,2,0:T(2,128)(2,1)}), bf16[2048,2,3,128]{3,1,2,0:T(2,128)(2,1)}) %all-gather.2.cloned.1.call-update) | async-done | bytes 3145744 | tf_op jit(solution)/shard_map/all_gather | solution.py:73
  521.1 3.4 gather_fusion.1
  524.5 1.5 fusion.17
  525.9 2.1 fusion.39
  529.2 2.5 multiply_add_fusion
  531.7 3.6 broadcast_select_fusion
  535.3 91.7 %all-to-all-start = ((bf16[4,64,3,3,2,128]{5,4,3,2,1,0:T(2,128)(2,1)}), bf16[4,64,3,3,2,128]{5,4,3,2,1,0:T(2,128)(2,1)S(1)}, u32[]{:S(2)}, u32[]{:S(2)}) async-start(bf16[4,64,3,3,2,128]{5,4,3,2,1,0:T(2,128)(2,1)} %broadcast_select_fusion), calls=%async_computation | async-start | bytes 2359296 | tf_op jit(solution)/shard_map/all_to_all | solution.py:105
  626.9 8.4 %multiply_convert_fusion.2 = bf16[512,1024]{1,0:T(8,128)(2,1)S(1)} fusion(s32[512]{0:T(512)S(1)} %multiply_add_fusion.1), kind=kLoop, calls=%fused_computation.14 | loop fusion | flops 8388608 | bytes 1050624 | tf_op jit(solution)/shard_map/convert_element_type | solution.py:95
  635.3 9.1 %fusion.7 = bf16[512,1024]{1,0:T(8,128)(2,1)} fusion(s32[512]{0:T(512)S(1)} %multiply_add_fusion.1), kind=kLoop, calls=%fused_computation.29 | loop fusion | flops 9961472 | bytes 1050624 | tf_op jit(solution)/shard_map/neg | solution.py:96
  644.5 1.5 copy.141
  646.8 4.9 convolution_convert_fusion
  652.6 3.6 copy.143
  656.2 2.9 reshape.317
  659.1 4.9 all-to-all-start.1
  665.6 14.9 %all-to-all-done.1 = bf16[4,2,73728]{2,1,0:T(2,128)(2,1)S(1)} async-done(((bf16[4,2,73728]{2,1,0:T(2,128)(2,1)}), bf16[4,2,73728]{2,1,0:T(2,128)(2,1)S(1)}, u32[]{:S(2)}, u32[]{:S(2)}) %all-to-all-start.1) | async-done | bytes 1179680 | tf_op jit(solution)/shard_map/all_to_all | solution.py:119
  680.5 7.7 all-to-all-start.2
  688.3 1.6 reshape.318
  689.8 3.1 copy.144
  693.0 1.8 copy.145
  697.5 1.6 pad_maximum_fusion.6
  699.1 2.9 all-to-all-done.2
  702.0 13.4 %all-to-all-start.3 = ((bf16[128,2,2,3,128]{4,2,3,1,0:T(2,128)(2,1)}), bf16[128,2,2,3,128]{4,2,3,1,0:T(2,128)(2,1)S(1)}, u32[]{:S(2)}, u32[]{:S(2)}) async-start(bf16[128,2,2,3,128]{4,2,3,1,0:T(2,128)(2,1)} %pad_maximum_fusion.6), calls=%async_computation.3 | async-start | bytes 786432 | tf_op jit(solution)/shard_map/all_to_all | solution.py:134
  715.4 2.1 cosine_multiply_fusion
  717.6 1.6 reduce.7
  719.6 21.0 %all-to-all-done.3 = bf16[128,2,2,3,128]{4,2,3,1,0:T(2,128)(2,1)S(1)} async-done(((bf16[128,2,2,3,128]{4,2,3,1,0:T(2,128)(2,1)}), bf16[128,2,2,3,128]{4,2,3,1,0:T(2,128)(2,1)S(1)}, u32[]{:S(2)}, u32[]{:S(2)}) %all-to-all-start.3) | async-done | bytes 393248 | tf_op jit(solution)/shard_map/all_to_all | solution.py:134
  741.9 1.5 convolution_multiply_fusion
  743.4 34.5 %reduce-scatter.2.cloned.1.call-done = f32[256,3,16]{0,2,1:T(8,128)} async-done(((f32[1024,3,16]{0,2,1:T(8,128)}), f32[256,3,16]{0,2,1:T(8,128)}) %reduce-scatter.2.cloned.1.call-update) | async-done | bytes 49168 | tf_op jit(solution)/shard_map/reduce_scatter | solution.py:165
  (81 shorter events, 19.7 us)
Async XLA Ops:
  6.5 514.5 %all-gather.2.cloned.1.call-start = ((), (), s32[]{:S(2)}) async-start(), calls=%async_computation.5 | async-start | bytes 3170304 | tf_op jit(solution)/shard_map/all_gather | solution.py:73
  17.2 3.7 copy-start.8
  528.0 1.0 copy-start
  528.0 1.2 copy-start.1
  535.3 109.2 %all-to-all-start = ((bf16[4,64,3,3,2,128]{5,4,3,2,1,0:T(2,128)(2,1)}), bf16[4,64,3,3,2,128]{5,4,3,2,1,0:T(2,128)(2,1)S(1)}, u32[]{:S(2)}, u32[]{:S(2)}) async-start(bf16[4,64,3,3,2,128]{5,4,3,2,1,0:T(2,128)(2,1)} %broadcast_select_fusion), calls=%async_computation | async-start | bytes 2359296 | tf_op jit(solution)/shard_map/all_to_all | solution.py:105
  656.2 7.8 copy-start.5
  659.1 5.7 copy-start.4
  659.1 21.4 %all-to-all-start.1 = ((bf16[4,2,73728]{2,1,0:T(2,128)(2,1)}), bf16[4,2,73728]{2,1,0:T(2,128)(2,1)S(1)}, u32[]{:S(2)}, u32[]{:S(2)}) async-start(bf16[4,2,73728]{2,1,0:T(2,128)(2,1)} %reshape.317), calls=%async_computation.1 | async-start | bytes 2359296 | tf_op jit(solution)/shard_map/all_to_all | solution.py:119
  680.5 21.4 %all-to-all-start.2 = ((s32[128,1,2]{2,1,0:T(1,128)}), s32[128,1,2]{2,1,0:T(1,128)}, u32[]{:S(2)}, u32[]{:S(2)}) async-start(s32[128,1,2]{2,1,0:T(1,128)} %bitcast.22), calls=%async_computation.2 | async-start | bytes 131072 | tf_op jit(solution)/shard_map/all_to_all | solution.py:137
  694.8 1.0 copy-start.2
  694.8 1.1 copy-start.3
  694.8 1.2 copy-start.6
  694.8 1.3 copy-start.7
  702.0 38.7 %all-to-all-start.3 = ((bf16[128,2,2,3,128]{4,2,3,1,0:T(2,128)(2,1)}), bf16[128,2,2,3,128]{4,2,3,1,0:T(2,128)(2,1)S(1)}, u32[]{:S(2)}, u32[]{:S(2)}) async-start(bf16[128,2,2,3,128]{4,2,3,1,0:T(2,128)(2,1)} %pad_maximum_fusion.6), calls=%async_computation.3 | async-start | bytes 786432 | tf_op jit(solution)/shard_map/all_to_all | solution.py:134
  715.4 62.5 %reduce-scatter.2.cloned.1.call-start = ((), (), s32[]{:S(2)}) async-start(), calls=%async_computation.6 | async-start | bytes 245760 | tf_op jit(solution)/shard_map/reduce_scatter | solution.py:165
Sparse Core Ops, SparseCore 0:
  9.4 511.5 all-gather.1
  743.5 34.2 reduce-scatter.1
where the time goes:
time: 786 us; the launch traced here: 785 us
  waiting for transfers between devices  567 us (72%)
  starting transfers between devices  118 us (15%)
  local copies, waits for them, and re-layouts  46.3 us (6%)
  other arithmetic  32.8 us (4%)
  between operations  13.8 us (2%)
    all_gather x1, waiting for transfers between devices, local(): part_rows = lax.all_gather(spec_rows, 'blk', axis=0, tiled=True)  494 us
    all_to_all x1, starting transfers between devices, local(): lax.all_to_all(sent, 'frq', split_axis=0, concat_axis=5, tiled=True)  91.7 us
    reduce_scatter x1, waiting for transfers between devices, local(): lax.psum_scatter(product.reshape(NT // band_total * lax.axis_size('frq'),...  34.5 us
    all_to_all x1, waiting for transfers between devices, local(): lax.all_to_all(far_block.astype(jnp.bfloat16), 'blk', split_axis=0, conca...  21 us
  transfers between devices with their start and end apart: 6, of which 5 were waited for; matrix products, arithmetic and copies ran while one was open for 7% of the time, Pallas kernels for 0%

commit v1 on v0

--- a/solution.py
+++ b/solution.py
@@ -70,7 +70,10 @@
         .astype(jnp.float32)
     )
     own_rows = jnp.take(spec_rows, own_ids, axis=0)
-    part_rows = lax.all_gather(spec_rows, "blk", axis=0, tiled=True)
+    count = lax.axis_size("blk")
+    tiles = jnp.stack([spec_rows for _ in range(count)])
+    tiles = lax.all_to_all(tiles, "blk", split_axis=0, concat_axis=0)
+    part_rows = jnp.concatenate(tiles, axis=0)
     first_row = jnp.int32(0)
     row_count = part_rows.shape[0]
     block_span = min(block_total, -(-row_count // per_block) + 1)

time: 786 us -> 360 us (0.46)
  waiting for transfers between devices: 567 us -> 195 us
  starting transfers between devices: 118 us -> 58.9 us
    all_gather x1 -> x0, waiting for transfers between devices: 494 us -> none  [local(): part_rows = lax.all_gather(spec_rows, 'blk', axis=0, tiled=True)]
    all_to_all x0 -> x1, waiting for transfers between devices: none -> 122 us  [local(): tiles = lax.all_to_all(tiles, 'blk', split_axis=0, concat_axis=0)]
    all_to_all x1, starting transfers between devices: 91.7 us -> 10 us  [local(): lax.all_to_all(sent, 'frq', split_axis=0, concat_axis=5, tiled=True)]
    all_to_all x0 -> x1, starting transfers between devices: none -> 22.4 us  [local(): tiles = lax.all_to_all(tiles, 'blk', split_axis=0, concat_axis=0)]
  transfers between devices with their start and end apart: 6 -> 6, of which waited for: 5 -> 5; matrix products, arithmetic and copies ran while one was open for 7% -> 14% of each run, Pallas kernels for 0% -> 0%
where the time goes in v1:
time: 360 us; the launch traced here: 356 us
  waiting for transfers between devices  195 us (54%)
  starting transfers between devices  58.9 us (16%)
  local copies, waits for them, and re-layouts  47 us (13%)
  other arithmetic  33 us (9%)
  between operations  14.1 us (4%)
  matrix products  7 us (2%)
    all_to_all x1, waiting for transfers between devices, local(): tiles = lax.all_to_all(tiles, 'blk', split_axis=0, concat_axis=0)  122 us
    reduce_scatter x1, waiting for transfers between devices, local(): lax.psum_scatter(product.reshape(NT // band_total * lax.axis_size('frq'),...  34.5 us
    all_to_all x1, starting transfers between devices, local(): tiles = lax.all_to_all(tiles, 'blk', split_axis=0, concat_axis=0)  22.4 us
    all_to_all x1, waiting for transfers between devices, local(): lax.all_to_all(far_block.astype(jnp.bfloat16), 'blk', split_axis=0, conca...  20.9 us
    all_to_all x1, waiting for transfers between devices, local(): lax.all_to_all(adjoint_rows, 'frq', split_axis=5, concat_axis=0, tiled=True)  14.9 us
    all_to_all x1, starting transfers between devices, local(): lax.all_to_all(far_block.astype(jnp.bfloat16), 'blk', split_axis=0, conca...  13.5 us
    all_to_all x1, starting transfers between devices, local(): lax.all_to_all(sent, 'frq', split_axis=0, concat_axis=5, tiled=True)  10 us
    neg x1, other arithmetic, local(): -(jnp.sin(phase) / math.sqrt(NF)).astype(jnp.bfloat16)  9.12 us
  transfers between devices with their start and end apart: 6, of which 5 were waited for; matrix products, arithmetic and copies ran while one was open for 14% of the time, Pallas kernels for 0%

profile of v1, /device:TPU:1, one launch (start us, length us, event | category | flops | bytes accessed | tf_op | source)
XLA Modules:
  0.0 355.5 jit_solution(6561156362725563043)
XLA Ops:
  7.3 3.3 stack.16
  10.6 22.4 %all-to-all-start = ((bf16[128,16,2,3,128]{4,2,3,1,0:T(2,128)(2,1)}), bf16[128,16,2,3,128]{4,2,3,1,0:T(2,128)(2,1)}, u32[]{:S(2)}, u32[]{:S(2)}) async-start(bf16[128,16,2,3,128]{4,2,3,1,0:T(2,128)(2,1)} %stack.16), calls=%async_computation | async-start | bytes 6291456 | tf_op jit(solution)/shard_map/all_to_all | solution.py:75
  37.1 1.5 gather_fusion
  45.6 2.3 copy.143
  47.9 2.6 reshape.286
  50.6 122.0 %all-to-all-done = bf16[128,16,2,3,128]{4,2,3,1,0:T(2,128)(2,1)} async-done(((bf16[128,16,2,3,128]{4,2,3,1,0:T(2,128)(2,1)}), bf16[128,16,2,3,128]{4,2,3,1,0:T(2,128)(2,1)}, u32[]{:S(2)}, u32[]{:S(2)}) %all-to-all-start) | async-done | bytes 3145760 | tf_op jit(solution)/shard_map/all_to_all | solution.py:75
  172.6 3.4 gather_fusion.1
  176.0 1.5 fusion.17
  177.5 2.1 fusion.39
  180.8 2.5 multiply_add_fusion
  183.3 3.6 %broadcast_select_fusion = bf16[4,64,3,3,2,128]{5,4,3,2,1,0:T(2,128)(2,1)} fusion(pred[4,64]{1,0:T(4,128)(4,1)S(1)} %compare_and_fusion.3, f32[4,64]{1,0:T(4,128)S(1)} %compare_convert_fusion, f32[4,64,3,3,1,128]{5,4,3,2,1,0:T(1,128)S(1)} %get-tuple-element.14, f32[4,64,3,3,1,128]{5,4,3,2,1,0:T(1,128)S(1)} %get-tuple-element.13), kind=kLoop, calls=%fused_computation.8 | loop fusion | flops 2359296 | bytes 3540224 | tf_op jit(solution)/shard_map/jit(_where)/select_n | solution.py:93
  186.8 10.0 %all-to-all-start.1 = ((bf16[4,64,3,3,2,128]{5,4,3,2,1,0:T(2,128)(2,1)}), bf16[4,64,3,3,2,128]{5,4,3,2,1,0:T(2,128)(2,1)S(1)}, u32[]{:S(2)}, u32[]{:S(2)}) async-start(bf16[4,64,3,3,2,128]{5,4,3,2,1,0:T(2,128)(2,1)} %broadcast_select_fusion), calls=%async_computation.1 | async-start | bytes 2359296 | tf_op jit(solution)/shard_map/all_to_all | solution.py:108
  196.9 8.4 %multiply_convert_fusion.2 = bf16[512,1024]{1,0:T(8,128)(2,1)S(1)} fusion(s32[512]{0:T(512)S(1)} %multiply_add_fusion.1), kind=kLoop, calls=%fused_computation.14 | loop fusion | flops 8388608 | bytes 1050624 | tf_op jit(solution)/shard_map/convert_element_type | solution.py:98
  205.3 9.1 %fusion.7 = bf16[512,1024]{1,0:T(8,128)(2,1)} fusion(s32[512]{0:T(512)S(1)} %multiply_add_fusion.1), kind=kLoop, calls=%fused_computation.29 | loop fusion | flops 9961472 | bytes 1050624 | tf_op jit(solution)/shard_map/neg | solution.py:99
  214.4 1.5 copy.142
  216.8 4.9 %convolution_convert_fusion = bf16[576,1024]{1,0:T(8,128)(2,1)S(1)} fusion(bf16[512,1024]{1,0:T(8,128)(2,1)} %fusion.7, bf16[512,1024]{1,0:T(8,128)(2,1)S(1)} %multiply_convert_fusion.2, f32[576,1024]{1,0:T(8,128)} %reshape.286, bf16[576,1024]{1,0:T(8,128)(2,1)S(1)} %reshape.280, f32[1024]{0:T(1024)S(1)} %fusion.25, f32[576]{0:T(1024)S(1)} %mul.323), kind=kOutput, calls=%fused_computation.18 | convolution fusion | flops 2427256832 | bytes 6822144 | tf_op jit(solution)/shard_map/dot_general | solution.py:116
  222.6 3.6 %copy.144 = bf16[1,64,3,3,2,512]{1,4,3,2,0,5:T(2,128)(2,1)S(1)} copy(bf16[1,64,3,3,2,512]{5,4,3,2,1,0:T(2,128)(2,1)S(1)} %reshape.281) | data formatting | bytes 2359296 | tf_op jit(solution)/shard_map/reshape | solution.py:120
  226.2 2.9 reshape.323
  229.0 4.9 %all-to-all-start.2 = ((bf16[4,2,73728]{2,1,0:T(2,128)(2,1)}), bf16[4,2,73728]{2,1,0:T(2,128)(2,1)S(1)}, u32[]{:S(2)}, u32[]{:S(2)}) async-start(bf16[4,2,73728]{2,1,0:T(2,128)(2,1)} %reshape.323), calls=%async_computation.2 | async-start | bytes 2359296 | tf_op jit(solution)/shard_map/all_to_all | solution.py:122
  235.5 14.9 %all-to-all-done.2 = bf16[4,2,73728]{2,1,0:T(2,128)(2,1)S(1)} async-done(((bf16[4,2,73728]{2,1,0:T(2,128)(2,1)}), bf16[4,2,73728]{2,1,0:T(2,128)(2,1)S(1)}, u32[]{:S(2)}, u32[]{:S(2)}) %all-to-all-start.2) | async-done | bytes 1179680 | tf_op jit(solution)/shard_map/all_to_all | solution.py:122
  250.5 8.0 %all-to-all-start.3 = ((s32[128,1,2]{2,1,0:T(1,128)}), s32[128,1,2]{2,1,0:T(1,128)}, u32[]{:S(2)}, u32[]{:S(2)}) async-start(s32[128,1,2]{2,1,0:T(1,128)} %bitcast.23), calls=%async_computation.3 | async-start | bytes 131072 | tf_op jit(solution)/shard_map/all_to_all | solution.py:140
  258.5 1.6 reshape.324
  260.0 3.1 copy.145
  263.1 1.8 copy.146
  267.6 1.6 pad_maximum_fusion.6
  269.3 3.1 all-to-all-done.3
  272.4 13.5 %all-to-all-start.4 = ((bf16[128,2,2,3,128]{4,2,3,1,0:T(2,128)(2,1)}), bf16[128,2,2,3,128]{4,2,3,1,0:T(2,128)(2,1)S(1)}, u32[]{:S(2)}, u32[]{:S(2)}) async-start(bf16[128,2,2,3,128]{4,2,3,1,0:T(2,128)(2,1)} %pad_maximum_fusion.6), calls=%async_computation.4 | async-start | bytes 786432 | tf_op jit(solution)/shard_map/all_to_all | solution.py:137
  286.0 2.1 cosine_multiply_fusion
  288.2 1.7 reduce.7
  290.3 20.9 %all-to-all-done.4 = bf16[128,2,2,3,128]{4,2,3,1,0:T(2,128)(2,1)S(1)} async-done(((bf16[128,2,2,3,128]{4,2,3,1,0:T(2,128)(2,1)}), bf16[128,2,2,3,128]{4,2,3,1,0:T(2,128)(2,1)S(1)}, u32[]{:S(2)}, u32[]{:S(2)}) %all-to-all-start.4) | async-done | bytes 393248 | tf_op jit(solution)/shard_map/all_to_all | solution.py:137
  312.5 1.5 convolution_multiply_fusion
  314.0 34.5 %reduce-scatter.2.cloned.1.call-done = f32[256,3,16]{0,2,1:T(8,128)} async-done(((f32[1024,3,16]{0,2,1:T(8,128)}), f32[256,3,16]{0,2,1:T(8,128)}) %reduce-scatter.2.cloned.1.call-update) | async-done | bytes 49168 | tf_op jit(solution)/shard_map/reduce_scatter | solution.py:168
  (85 shorter events, 20.7 us)
Async XLA Ops:
  10.6 22.4 %copy-start.8 = (s32[1,128,2]{1,2,0:T(2,128)S(1)}, s32[1,128,2]{1,2,0:T(2,128)}, u32[]{:S(2)}) copy-start(s32[1,128,2]{1,2,0:T(2,128)} %param.8) | copy-start | bytes 3076
  10.6 25.1 %copy-start.9 = (s32[1,128,2]{1,2,0:T(2,128)S(1)}, s32[1,128,2]{1,2,0:T(2,128)}, u32[]{:S(2)}) copy-start(s32[1,128,2]{1,2,0:T(2,128)} %param.7) | copy-start | bytes 3076
  10.6 162.0 %all-to-all-start = ((bf16[128,16,2,3,128]{4,2,3,1,0:T(2,128)(2,1)}), bf16[128,16,2,3,128]{4,2,3,1,0:T(2,128)(2,1)}, u32[]{:S(2)}, u32[]{:S(2)}) async-start(bf16[128,16,2,3,128]{4,2,3,1,0:T(2,128)(2,1)} %stack.16), calls=%async_computation | async-start | bytes 6291456 | tf_op jit(solution)/shard_map/all_to_all | solution.py:75
  40.2 3.7 %copy-start.10 = (s32[1,128]{1,0:T(1,128)S(1)}, s32[1,128]{1,0:T(1,128)}, u32[]{:S(2)}) copy-start(s32[1,128]{1,0:T(1,128)} %param.9) | copy-start | bytes 1540
  179.6 1.0 copy-start
  179.6 1.2 copy-start.1
  186.8 27.6 %all-to-all-start.1 = ((bf16[4,64,3,3,2,128]{5,4,3,2,1,0:T(2,128)(2,1)}), bf16[4,64,3,3,2,128]{5,4,3,2,1,0:T(2,128)(2,1)S(1)}, u32[]{:S(2)}, u32[]{:S(2)}) async-start(bf16[4,64,3,3,2,128]{5,4,3,2,1,0:T(2,128)(2,1)} %broadcast_select_fusion), calls=%async_computation.1 | async-start | bytes 2359296 | tf_op jit(solution)/shard_map/all_to_all | solution.py:108
  226.2 7.8 %copy-start.5 = (f32[256,1,3,128]{3,1,2,0:T(1,128)S(1)}, f32[256,1,3,128]{3,1,2,0:T(1,128)}, u32[]{:S(2)}) copy-start(f32[256,1,3,128]{3,1,2,0:T(1,128)} %get-tuple-element.16) | copy-start | bytes 1179652
  229.0 5.7 %copy-start.4 = (f32[256,1,3,128]{3,1,2,0:T(1,128)S(1)}, f32[256,1,3,128]{3,1,2,0:T(1,128)}, u32[]{:S(2)}) copy-start(f32[256,1,3,128]{3,1,2,0:T(1,128)} %get-tuple-element.15) | copy-start | bytes 1179652
  229.0 21.4 %all-to-all-start.2 = ((bf16[4,2,73728]{2,1,0:T(2,128)(2,1)}), bf16[4,2,73728]{2,1,0:T(2,128)(2,1)S(1)}, u32[]{:S(2)}, u32[]{:S(2)}) async-start(bf16[4,2,73728]{2,1,0:T(2,128)(2,1)} %reshape.323), calls=%async_computation.2 | async-start | bytes 2359296 | tf_op jit(solution)/shard_map/all_to_all | solution.py:122
  250.5 21.9 %all-to-all-start.3 = ((s32[128,1,2]{2,1,0:T(1,128)}), s32[128,1,2]{2,1,0:T(1,128)}, u32[]{:S(2)}, u32[]{:S(2)}) async-start(s32[128,1,2]{2,1,0:T(1,128)} %bitcast.23), calls=%async_computation.3 | async-start | bytes 131072 | tf_op jit(solution)/shard_map/all_to_all | solution.py:140
  265.0 1.0 copy-start.2
  265.0 1.1 copy-start.3
  265.0 1.2 copy-start.6
  265.0 1.3 copy-start.7
  272.4 38.8 %all-to-all-start.4 = ((bf16[128,2,2,3,128]{4,2,3,1,0:T(2,128)(2,1)}), bf16[128,2,2,3,128]{4,2,3,1,0:T(2,128)(2,1)S(1)}, u32[]{:S(2)}, u32[]{:S(2)}) async-start(bf16[128,2,2,3,128]{4,2,3,1,0:T(2,128)(2,1)} %pad_maximum_fusion.6), calls=%async_computation.4 | async-start | bytes 786432 | tf_op jit(solution)/shard_map/all_to_all | solution.py:137
  285.9 62.5 %reduce-scatter.2.cloned.1.call-start = ((), (), s32[]{:S(2)}) async-start(), calls=%async_computation.6 | async-start | bytes 245760 | tf_op jit(solution)/shard_map/reduce_scatter | solution.py:168
Sparse Core Ops, SparseCore 0:
  314.1 34.2 reduce-scatter.1
